TPU v7x, 32 devices: a whole 2x2x4 slice. The times are simulated.
32 devices in a mesh: src: 2 (over core), rows: 16 (over z, y, x).
Axes of the slice: x: 2, y: 2, z: 4, core: 2. Of those that a mesh axis runs over, the one named last changes fastest.
Arguments:
- slip_units: int32 [512, 2000], P(None, 'src'), may hold values from 0 to 15
- slip_scales: float32 [512, 16], P(None, 'src'), may hold values from 0.02 to 0.2
- green: bfloat16 [2000, 491520], P('src', 'rows'), may hold values from -0.08944272 to 0.08944272
- coast_gauges: int32 [2048, 8], replicated, may hold values from 0 to 2047
- coast_amps: float32 [2048, 8], replicated, may hold values from 0.05 to 0.3
- coast_counts: int32 [2048], replicated, may hold values from 1 to 8
Outputs:
- onshore: float32 [512, 2048], P('src', 'rows')
Inputs may be any that keep to these rules, and one draw needn't show every extreme that they name: coast_gauges names gauges.
All inputs are finite; a program needn't handle non-finite values.
Results may differ from a plain program's by a relative error of at most 0.0039.
Values may be sent and summed in bfloat16 or wider, within the bound.
No kernel may reach another device: no remote copies, remote signals or barrier semaphores. Data moves between devices by JAX's collectives and lax.ppermute only.
A program may use at most 192 MiB of HBM per device.

v0:
```python
import jax
import jax.numpy as jnp
from jax import lax
from jax.sharding import PartitionSpec as P

NT = 240
UBLK = 125


def body(slip_units, slip_scales, green, coast_gauges, coast_amps, coast_counts):
    scenarios = slip_units.shape[0]
    sources_here = slip_units.shape[1]
    block_count = slip_scales.shape[1]
    slip_weights = (
        (
            slip_units.astype(jnp.float32).reshape(scenarios, block_count, UBLK)
            * slip_scales[:, :, None]
        )
        .reshape(scenarios, sources_here)
        .astype(jnp.bfloat16)
    )
    columns = green.shape[1]
    gauge_count = columns // NT
    groups = lax.axis_size("src")
    portion = scenarios // groups
    waveforms = lax.psum_scatter(
        jnp.dot(slip_weights, green, preferred_element_type=jnp.float32).astype(jnp.bfloat16),
        "src",
        scatter_dimension=0,
        tiled=True,
    ).astype(jnp.float32)
    peak_values = jnp.max(jnp.abs(waveforms.reshape(portion, gauge_count, NT)), axis=2)
    tile_total = coast_gauges.shape[0]
    slot_count = coast_gauges.shape[1]
    owners = lax.axis_size("rows")
    tiles_here = tile_total // owners
    active_slot = jnp.arange(slot_count, dtype=jnp.int32)[None, :] < coast_counts[:, None]
    weights = jnp.where(active_slot, coast_amps, jnp.zeros_like(coast_amps))
    gathered = lax.all_gather(peak_values, "rows", axis=1, tiled=True)
    first_tile = lax.axis_index("rows") * tiles_here
    mine_gauges = lax.dynamic_slice_in_dim(coast_gauges, first_tile, tiles_here, 0)
    mine_weights = lax.dynamic_slice_in_dim(weights, first_tile, tiles_here, 0)
    matches = (
        mine_gauges[:, :, None] == jnp.arange(gauge_count * owners, dtype=jnp.int32)[None, None, :]
    )
    tile_table = jnp.sum(jnp.where(matches, mine_weights[:, :, None], 0.0), axis=1)
    onshore = lax.dot_general(
        gathered,
        tile_table,
        (((1,), (1,)), ((), ())),
        precision=lax.Precision.HIGHEST,
        preferred_element_type=jnp.float32,
    )
    return onshore


def solution(mesh):
    in_specs = (P(None, "src"), P(None, "src"), P("src", "rows"), P(), P(), P())
    out_specs = P("src", "rows")
    return jax.shard_map(body, mesh=mesh, in_specs=in_specs, out_specs=out_specs, check_vma=False)
```

profile of v0, /device:TPU:0, one launch (start us, length us, event | category | flops | bytes accessed | tf_op | source)
XLA Modules:
  0.0 232.7 jit_solution(9461021766356233926)
XLA Ops:
  6.5 0.0 copy-start
  6.5 0.0 reduce-scatter.2.cloned.1.call-start
  6.5 1.0 mul.14
  7.5 1.6 mul.15
  9.1 43.3 %convolution_convert_fusion = bf16[512,30720]{1,0:T(8,128)(2,1)} fusion(bf16[1000,30720]{1,0:T(8,128)(2,1)} %param.8, f32[512,1000]{0,1:T(8,128)} %mul.15, s32[512,1000]{0,1:T(8,128)} %param.6), kind=kOutput, calls=%fused_computation | convolution fusion | flops 31474544640 | bytes 96993280 | tf_op jit(solution)/shard_map/dot_general | solution.py:27
  52.4 0.0 reduce-scatter.2.cloned.1.call-update
  52.4 0.2 all-gather.2.cloned.1.call-start
  52.6 45.3 %reduce-scatter.2.cloned.1.call-done = bf16[256,30720]{1,0:T(8,128)(2,1)} async-done(((bf16[512,30720]{1,0:T(8,128)(2,1)}), bf16[256,30720]{1,0:T(8,128)(2,1)}) %reduce-scatter.2.cloned.1.call-update) | async-done | bytes 15728656 | tf_op jit(solution)/shard_map/reduce_scatter | solution.py:26
  97.9 17.5 %convert_abs_fusion = f32[256,30720]{1,0:T(8,128)} fusion(bf16[256,30720]{1,0:T(8,128)(2,1)} %reduce-scatter.2.cloned.1.call-done), kind=kLoop, calls=%fused_computation.1 | loop fusion | flops 15728640 | bytes 47185920 | tf_op jit(solution)/shard_map/abs | solution.py:32
  115.5 30.7 %copy.15 = f32[256,30720]{0,1:T(8,128)} copy(f32[256,30720]{1,0:T(8,128)} %convert_abs_fusion) | data formatting | bytes 62914560 | tf_op jit(solution)/shard_map/abs | solution.py:32
  146.1 12.0 %reduce_max.9 = f32[256,128]{0,1:T(8,128)} reduce(f32[256,128,240]{0,2,1:T(8,128)} %bitcast.7, f32[]{:T(128)} %constant.6.clone.1), dimensions={2}, to_apply=%region_1.0 | reduce | flops 7831552 | bytes 31588356 | tf_op jit(solution)/shard_map/reduce_max | solution.py:32
  158.1 0.0 all-gather.2.cloned.1.call-update
  158.1 0.8 dynamic-slice
  158.9 0.7 dynamic-slice_select_fusion
  159.6 0.1 copy.17
  159.7 0.0 copy-done
  159.7 0.1 copy.16
  159.8 2.7 %select_reduce_fusion = f32[128,2048]{1,0:T(8,128)S(1)} fusion(f32[128,8]{1,0:T(8,128)S(1)} %copy.17, s32[128,8]{1,0:T(8,128)S(1)} %copy.16), kind=kLoop, calls=%fused_computation.2 | loop fusion | flops 6029312 | bytes 1056768 | tf_op jit(solution)/shard_map/reduce_sum | solution.py:46
  162.6 57.6 %all-gather.2.cloned.1.call-done = f32[256,2048]{0,1:T(8,128)} async-done(((f32[256,128]{0,1:T(8,128)}), f32[256,2048]{0,1:T(8,128)}) %all-gather.2.cloned.1.call-update) | async-done | bytes 2097168 | tf_op jit(solution)/shard_map/all_gather | solution.py:39
  220.2 5.7 %fusion = f32[256,128]{1,0:T(8,128)} fusion(f32[256,2048]{0,1:T(8,128)} %all-gather.2.cloned.1.call-done, f32[128,2048]{1,0:T(8,128)S(1)} %select_reduce_fusion), kind=kOutput, calls=%fused_computation.8 | convolution fusion | flops 805306368 | bytes 3276800 | tf_op jit(solution)/shard_map/dot_general | solution.py:47
  (1 shorter events, 0.0 us)
Async XLA Ops:
  6.5 153.2 %copy-start = (s32[2048,8]{0,1:T(8,128)S(1)}, s32[2048,8]{0,1:T(8,128)}, u32[]{:S(2)}) copy-start(s32[2048,8]{0,1:T(8,128)} %param.9) | copy-start | bytes 196612
  6.5 91.4 %reduce-scatter.2.cloned.1.call-start = ((), (), s32[]{:S(2)}) async-start(), calls=%async_computation.1 | async-start | bytes 47185920 | tf_op jit(solution)/shard_map/reduce_scatter | solution.py:26
  52.4 167.7 %all-gather.2.cloned.1.call-start = ((), (), s32[]{:S(2)}) async-start(), calls=%async_computation.2 | async-start | bytes 2228224 | tf_op jit(solution)/shard_map/all_gather | solution.py:39
Sparse Core Ops, SparseCore 0:
  52.5 45.3 reduce-scatter.1
  158.3 61.8 all-gather.1
where the time goes:
time: 233 us
  waiting for transfers between devices  103 us (44%)
  matrix products  48.9 us (21%)
  local copies, waits for them, and re-layouts  34.2 us (15%)
  other arithmetic  32.9 us (14%)
  between operations  13.4 us (6%)
    all_gather x1, waiting for transfers between devices, body(): gathered = lax.all_gather(peak_values, 'rows', axis=1, tiled=True)  57.6 us
    reduce_scatter x1, waiting for transfers between devices, body(): lax.psum_scatter(jnp.dot(slip_weights, green, preferred_element_type=jnp....  45.3 us
    dot_general x1, matrix products, body(): jnp.dot(slip_weights, green, preferred_element_type=jnp.float32)  43.3 us
    abs x1, local copies, waits for them, and re-layouts, body(): jnp.abs(waveforms.reshape(portion, gauge_count, NT))  30.7 us
    abs x1, other arithmetic, body(): jnp.abs(waveforms.reshape(portion, gauge_count, NT))  17.5 us
    reduce_max x1, other arithmetic, body(): jnp.max(jnp.abs(waveforms.reshape(portion, gauge_count, NT)), axis=2)  12 us
    dot_general x1, matrix products, body(): lax.dot_general(gathered, tile_table, (((1,), (1,)), ((), ())), precision...  5.67 us
  transfers between devices with their start and end apart: 2, of which 2 were waited for; matrix products, arithmetic and copies ran while one was open for 2% of the time, Pallas kernels for 0%

commit v1 on v0

--- a/solution.py
+++ b/solution.py
@@ -36,7 +36,18 @@
     tiles_here = tile_total // owners
     active_slot = jnp.arange(slot_count, dtype=jnp.int32)[None, :] < coast_counts[:, None]
     weights = jnp.where(active_slot, coast_amps, jnp.zeros_like(coast_amps))
-    gathered = lax.all_gather(peak_values, "rows", axis=1, tiled=True)
+    m_next = jax.lax.axis_size("rows")
+    t1 = jax.lax.axis_index("rows")
+    e_next, heard = (m_next, t1)
+    gathered, t_next = (peak_values, 1)
+    while t_next < e_next:
+        step_out = jax.lax.ppermute(
+            gathered, "rows", [(dev_i, dev_i ^ t_next) for dev_i in range(e_next)]
+        )
+        vec_out = jnp.concatenate([gathered, step_out], axis=1)
+        oldest = jnp.concatenate([step_out, gathered], 1)
+        gathered = jnp.where(heard & t_next == 0, vec_out, oldest)
+        t_next = 2 * t_next
     first_tile = lax.axis_index("rows") * tiles_here
     mine_gauges = lax.dynamic_slice_in_dim(coast_gauges, first_tile, tiles_here, 0)
     mine_weights = lax.dynamic_slice_in_dim(weights, first_tile, tiles_here, 0)

time: 233 us -> 242 us (1.039)
  starting transfers between devices: 0.22 us -> 8.02 us
    ppermute x0 -> x4, waiting for transfers between devices: none -> 59.6 us  [body(): jax.lax.ppermute(gathered, 'rows', [(dev_i, dev_i ^ t_next) for dev_i in...]
    all_gather x1 -> x0, waiting for transfers between devices: 57.6 us -> none  [body(): gathered = lax.all_gather(peak_values, 'rows', axis=1, tiled=True)]
    ppermute x0 -> x4, starting transfers between devices: none -> 8.02 us  [body(): jax.lax.ppermute(gathered, 'rows', [(dev_i, dev_i ^ t_next) for dev_i in...]
  transfers between devices with their start and end apart: 2 -> 5, of which waited for: 2 -> 5; matrix products, arithmetic and copies ran while one was open for 2% -> 2% of each run, Pallas kernels for 0% -> 0%
where the time goes in v1:
time: 242 us; the launch traced here: 241 us
  waiting for transfers between devices  105 us (43%)
  matrix products  47.4 us (20%)
  local copies, waits for them, and re-layouts  34.2 us (14%)
  other arithmetic  32.6 us (13%)
  between operations  13.5 us (6%)
  starting transfers between devices  8.02 us (3%)
    ppermute x4, waiting for transfers between devices, body(): jax.lax.ppermute(gathered, 'rows', [(dev_i, dev_i ^ t_next) for dev_i in...  59.6 us
    reduce_scatter x1, waiting for transfers between devices, body(): lax.psum_scatter(jnp.dot(slip_weights, green, preferred_element_type=jnp....  45.5 us
    dot_general x1, matrix products, body(): jnp.dot(slip_weights, green, preferred_element_type=jnp.float32)  43.3 us
    abs x1, local copies, waits for them, and re-layouts, body(): jnp.abs(waveforms.reshape(portion, gauge_count, NT))  30.7 us
    abs x1, other arithmetic, body(): jnp.abs(waveforms.reshape(portion, gauge_count, NT))  17.5 us
    reduce_max x1, other arithmetic, body(): jnp.max(jnp.abs(waveforms.reshape(portion, gauge_count, NT)), axis=2)  11.3 us
    ppermute x4, starting transfers between devices, body(): jax.lax.ppermute(gathered, 'rows', [(dev_i, dev_i ^ t_next) for dev_i in...  8.02 us
  transfers between devices with their start and end apart: 5, of which 5 were waited for; matrix products, arithmetic and copies ran while one was open for 2% of the time, Pallas kernels for 0%

profile of v1, /device:TPU:0, one launch (start us, length us, event | category | flops | bytes accessed | tf_op | source)
XLA Modules:
  0.0 240.9 jit_solution(12938783877304440868)
XLA Ops:
  6.5 0.0 copy-start
  6.5 0.0 reduce-scatter.2.cloned.1.call-start
  6.5 1.0 mul.14
  7.5 1.6 mul.15
  9.1 43.3 %convolution_convert_fusion = bf16[512,30720]{1,0:T(8,128)(2,1)} fusion(bf16[1000,30720]{1,0:T(8,128)(2,1)} %param.8, f32[512,1000]{0,1:T(8,128)} %mul.15, s32[512,1000]{0,1:T(8,128)} %param.6), kind=kOutput, calls=%fused_computation | convolution fusion | flops 31474544640 | bytes 96993280 | tf_op jit(solution)/shard_map/dot_general | solution.py:27
  52.4 0.0 reduce-scatter.2.cloned.1.call-update
  52.4 45.5 %reduce-scatter.2.cloned.1.call-done = bf16[256,30720]{1,0:T(8,128)(2,1)} async-done(((bf16[512,30720]{1,0:T(8,128)(2,1)}), bf16[256,30720]{1,0:T(8,128)(2,1)}) %reduce-scatter.2.cloned.1.call-update) | async-done | bytes 15728656 | tf_op jit(solution)/shard_map/reduce_scatter | solution.py:26
  97.9 17.5 %convert_abs_fusion = f32[256,30720]{1,0:T(8,128)} fusion(bf16[256,30720]{1,0:T(8,128)(2,1)} %reduce-scatter.2.cloned.1.call-done), kind=kLoop, calls=%fused_computation.1 | loop fusion | flops 15728640 | bytes 47185920 | tf_op jit(solution)/shard_map/abs | solution.py:32
  115.5 30.7 %copy.15 = f32[256,30720]{0,1:T(8,128)} copy(f32[256,30720]{1,0:T(8,128)} %convert_abs_fusion) | data formatting | bytes 62914560 | tf_op jit(solution)/shard_map/abs | solution.py:32
  146.1 11.3 %reduce_max.9 = f32[256,128]{0,1:T(8,128)S(1)} reduce(f32[256,128,240]{0,2,1:T(8,128)} %bitcast.6, f32[]{:T(128)} %constant.5.clone.1), dimensions={2}, to_apply=%region_1.0 | reduce | flops 7831552 | bytes 31588356 | tf_op jit(solution)/shard_map/reduce_max | solution.py:32
  157.5 1.8 collective-permute-start
  159.2 4.0 %collective-permute-done = f32[256,128]{0,1:T(8,128)S(1)} collective-permute-done((f32[256,128]{0,1:T(8,128)S(1)}, f32[256,128]{0,1:T(8,128)S(1)}, u32[]{:S(2)}, u32[]{:S(2)}) %collective-permute-start) | collective-permute-done | bytes 131104 | tf_op jit(solution)/shard_map/ppermute | solution.py:44
  163.3 1.8 collective-permute-start.1
  165.1 6.0 %collective-permute-done.1 = f32[256,256]{0,1:T(8,128)S(1)} collective-permute-done((f32[256,256]{0,1:T(8,128)S(1)}, f32[256,256]{0,1:T(8,128)S(1)}, u32[]{:S(2)}, u32[]{:S(2)}) %collective-permute-start.1) | collective-permute-done | bytes 262176 | tf_op jit(solution)/shard_map/ppermute | solution.py:44
  171.1 1.8 collective-permute-start.2
  172.9 10.7 %collective-permute-done.2 = f32[256,512]{0,1:T(8,128)S(1)} collective-permute-done((f32[256,512]{0,1:T(8,128)S(1)}, f32[256,512]{0,1:T(8,128)S(1)}, u32[]{:S(2)}, u32[]{:S(2)}) %collective-permute-start.2) | collective-permute-done | bytes 524320 | tf_op jit(solution)/shard_map/ppermute | solution.py:44
  183.6 0.1 maximum_select_fusion.2
  183.7 2.7 %collective-permute-start.3 = (f32[256,1024]{0,1:T(8,128)S(1)}, f32[256,1024]{0,1:T(8,128)S(1)}, u32[]{:S(2)}, u32[]{:S(2)}) collective-permute-start(f32[256,1024]{0,1:T(8,128)S(1)} %maximum_select_fusion.2), channel_id=1, source_target_pairs={{0,8},{1,9},{2,10},{3,11},{4,12},{5,13},{6,14},{7,15},{8,0},{9,1},... | collective-permute-start | bytes 3145736 | tf_op jit(solution)/shard_map/ppermute | solution.py:44
  186.4 0.8 dynamic-slice
  187.2 0.7 dynamic-slice_select_fusion
  187.9 0.1 copy.17
  188.0 0.0 copy-done
  188.0 0.1 copy.16
  188.1 2.9 %select_reduce_fusion = f32[128,2048]{1,0:T(8,128)S(1)} fusion(f32[128,8]{1,0:T(8,128)S(1)} %copy.17, s32[128,8]{1,0:T(8,128)S(1)} %copy.16), kind=kLoop, calls=%fused_computation.2 | loop fusion | flops 6029312 | bytes 1056768 | tf_op jit(solution)/shard_map/reduce_sum | solution.py:57
  191.0 38.9 %collective-permute-done.3 = f32[256,1024]{0,1:T(8,128)S(1)} collective-permute-done((f32[256,1024]{0,1:T(8,128)S(1)}, f32[256,1024]{0,1:T(8,128)S(1)}, u32[]{:S(2)}, u32[]{:S(2)}) %collective-permute-start.3) | collective-permute-done | bytes 1048608 | tf_op jit(solution)/shard_map/ppermute | solution.py:44
  229.9 4.1 %fusion = f32[256,128]{1,0:T(8,128)} fusion(f32[128,2048]{1,0:T(8,128)S(1)} %select_reduce_fusion, f32[256,1024]{0,1:T(8,128)S(1)} %collective-permute-done.3, f32[256,1024]{0,1:T(8,128)S(1)} %maximum_select_fusion.2, pred[]{:T(512)S(6)} %eq.25), kind=kOutput, calls=%fused_computation.5 | convolution fusion | flops 806879232 | bytes 3276801 | tf_op jit(solution)/shard_map/dot_general | solution.py:58
  (3 shorter events, 0.1 us)
Async XLA Ops:
  6.5 181.4 %copy-start = (s32[2048,8]{0,1:T(8,128)S(1)}, s32[2048,8]{0,1:T(8,128)}, u32[]{:S(2)}) copy-start(s32[2048,8]{0,1:T(8,128)} %param.9) | copy-start | bytes 196612
  6.5 91.4 %reduce-scatter.2.cloned.1.call-start = ((), (), s32[]{:S(2)}) async-start(), calls=%async_computation.1 | async-start | bytes 47185920 | tf_op jit(solution)/shard_map/reduce_scatter | solution.py:26
  157.5 5.8 %collective-permute-start = (f32[256,128]{0,1:T(8,128)S(1)}, f32[256,128]{0,1:T(8,128)S(1)}, u32[]{:S(2)}, u32[]{:S(2)}) collective-permute-start(f32[256,128]{0,1:T(8,128)S(1)} %reduce_max.9), channel_id=1, source_target_pairs={{0,1},{1,0},{2,3},{3,2},{4,5},{5,4},{6,7},{7,6},{8,9},{9,8},{10,11... | collective-permute-start | bytes 393224 | tf_op jit(solution)/shard_map/ppermute | solution.py:44
  163.3 7.8 %collective-permute-start.1 = (f32[256,256]{0,1:T(8,128)S(1)}, f32[256,256]{0,1:T(8,128)S(1)}, u32[]{:S(2)}, u32[]{:S(2)}) collective-permute-start(f32[256,256]{0,1:T(8,128)S(1)} %maximum_select_fusion.4), channel_id=1, source_target_pairs={{0,2},{1,3},{2,0},{3,1},{4,6},{5,7},{6,4},{7,5},{8,10},{9,11},{10,... | collective-permute-start | bytes 786440 | tf_op jit(solution)/shard_map/ppermute | solution.py:44
  171.1 12.5 %collective-permute-start.2 = (f32[256,512]{0,1:T(8,128)S(1)}, f32[256,512]{0,1:T(8,128)S(1)}, u32[]{:S(2)}, u32[]{:S(2)}) collective-permute-start(f32[256,512]{0,1:T(8,128)S(1)} %maximum_select_fusion.3), channel_id=1, source_target_pairs={{0,4},{1,5},{2,6},{3,7},{4,0},{5,1},{6,2},{7,3},{8,12},{9,13},{10,... | collective-permute-start | bytes 1572872 | tf_op jit(solution)/shard_map/ppermute | solution.py:44
  183.7 46.2 %collective-permute-start.3 = (f32[256,1024]{0,1:T(8,128)S(1)}, f32[256,1024]{0,1:T(8,128)S(1)}, u32[]{:S(2)}, u32[]{:S(2)}) collective-permute-start(f32[256,1024]{0,1:T(8,128)S(1)} %maximum_select_fusion.2), channel_id=1, source_target_pairs={{0,8},{1,9},{2,10},{3,11},{4,12},{5,13},{6,14},{7,15},{8,0},{9,1},... | collective-permute-start | bytes 3145736 | tf_op jit(solution)/shard_map/ppermute | solution.py:44
Sparse Core Ops, SparseCore 0:
  52.5 45.3 reduce-scatter.1
